TPU v7x, 32 devices: a whole 2x2x4 slice. The times are simulated.
32 devices in a mesh: seq: 8 (over z, y), fsdp: 4 (over x, core).
Axes of the slice: x: 2, y: 2, z: 4, core: 2. Of those that a mesh axis runs over, the one named last changes fastest.
Arguments:
- inputs: bfloat16 [12288, 1536], P(('seq', 'fsdp')), may hold values from -15 to 15
- layer_norm_gain: float32 [1536], replicated, may hold values from 0.25 to 1.75
- layer_norm_bias: float32 [1536], replicated, may hold values from -4 to 4
- w_in: bfloat16 [1536, 3072], P('fsdp'), may hold values from -0.15625 to 0.15625
- dw_kernel: float32 [32, 1536], replicated, may hold values from -1 to 1
- bn_gain: float32 [1536], replicated, may hold values from 0.25 to 1.75
- bn_bias: float32 [1536], replicated, may hold values from -4 to 4
- cotangent: bfloat16 [12288, 1536], P(('seq', 'fsdp')), may hold values from -6 to 6
Outputs:
- output: bfloat16 [12288, 1536], P(('seq', 'fsdp'))
- input_gradient: bfloat16 [12288, 1536], P(('seq', 'fsdp'))
- grad_w_in: float32 [1536, 3072], P('fsdp')
- grad_kernel: float32 [32, 1536], replicated
- grad_bn_gain: float32 [1536], replicated
- grad_bn_bias: float32 [1536], replicated
- layer_norm_gain_gradient: float32 [1536], replicated
- grad_ln_bias: float32 [1536], replicated
All inputs are finite; a program needn't handle non-finite values.
Results may differ from a plain program's by a relative error of at most 0.012.
The roundings to bfloat16 on the way count: a program that leaves them out, or rounds other values in their place, can miss the bound.
Values may be sent and summed in bfloat16 or wider, within the bound.
No kernel may reach another device: no remote copies, remote signals or barrier semaphores. Data moves between devices by JAX's collectives and lax.ppermute only.
A program may use at most 128 MiB of HBM per device.

v0:
```python
import jax
import jax.numpy as jnp
from jax import lax
from jax.sharding import PartitionSpec as P

epsilon = 1e-05


def from_behind(block, axis, distance):
    devices = range(lax.axis_size(axis))
    route = [(i - distance, i) for i in devices if i - distance in devices]
    return lax.ppermute(block, axis, route)


def on_device(
    inputs, layer_norm_gain, layer_norm_bias, w_in, dw_kernel, bn_gain, bn_bias, cotangent
):
    tok_rows = inputs.shape[0]
    features = inputs.shape[1]
    kernel_len = dw_kernel.shape[0]
    all_frames = tok_rows * lax.axis_size("seq") * lax.axis_size("fsdp")
    frames = inputs.astype(jnp.float32)
    row_mean = jnp.mean(frames, axis=-1, keepdims=True)
    centered_rows = frames - row_mean
    row_inverse_deviation = lax.rsqrt(
        jnp.mean(centered_rows * centered_rows, axis=-1, keepdims=True) + epsilon
    )
    standardized_input = centered_rows * row_inverse_deviation
    normalized_rows = (standardized_input * layer_norm_gain + layer_norm_bias).astype(jnp.bfloat16)
    full_weight = lax.all_gather(w_in, "fsdp", axis=0, tiled=True)
    hidden = jnp.dot(normalized_rows, full_weight, preferred_element_type=jnp.float32)
    value_part = hidden[:, :features]
    gate_sig = jax.nn.sigmoid(hidden[:, features:])
    glu = (value_part * gate_sig).astype(jnp.bfloat16)
    past_rim = from_behind(glu[tok_rows - (kernel_len - 1) :], ("seq", "fsdp"), 1)
    padded_glu = jnp.concatenate([past_rim, glu], axis=0).astype(jnp.float32)
    conv_out = jnp.zeros((tok_rows, features), jnp.float32)
    for offset in range(kernel_len):
        conv_out = (
            conv_out
            + dw_kernel[offset]
            * padded_glu[kernel_len - 1 - offset : kernel_len - 1 - offset + tok_rows]
        )
    chan_mean = lax.psum(jnp.sum(conv_out, axis=0), ("seq", "fsdp")) / all_frames
    conv_centred = conv_out - chan_mean
    chan_var = lax.psum(jnp.sum(conv_centred * conv_centred, axis=0), ("seq", "fsdp")) / all_frames
    bn_rstd = lax.rsqrt(chan_var + epsilon)
    chat = conv_centred * bn_rstd
    z_value = chat * bn_gain + bn_bias
    z_sig = jax.nn.sigmoid(z_value)
    output = (z_value * z_sig).astype(jnp.bfloat16)
    grad_z = cotangent.astype(jnp.float32) * z_sig * (1.0 + z_value * (1.0 - z_sig))
    grad_bn_bias, grad_bn_gain = lax.psum(
        (jnp.sum(grad_z, axis=0), jnp.sum(grad_z * chat, axis=0)), ("seq", "fsdp")
    )
    grad_conv = (
        bn_gain * bn_rstd * (grad_z - grad_bn_bias / all_frames - chat * grad_bn_gain / all_frames)
    )
    future_rim = from_behind(grad_conv[: kernel_len - 1], ("seq", "fsdp"), -1)
    padded_grad = jnp.concatenate([grad_conv, future_rim], axis=0)
    grad_glu = jnp.zeros((tok_rows, features), jnp.float32)
    kernel_rows = []
    for offset in range(kernel_len):
        grad_glu = grad_glu + dw_kernel[offset] * padded_grad[offset : offset + tok_rows]
        kernel_rows.append(
            jnp.sum(
                grad_conv
                * padded_glu[kernel_len - 1 - offset : kernel_len - 1 - offset + tok_rows],
                axis=0,
            )
        )
    kernel_portion = jnp.stack(kernel_rows, axis=0)
    grad_value = grad_glu * gate_sig
    grad_gate = grad_glu * value_part * gate_sig * (1.0 - gate_sig)
    grad_hidden = jnp.concatenate([grad_value, grad_gate], axis=1).astype(jnp.bfloat16)
    normalized_gradient = lax.dot_general(
        grad_hidden, full_weight, (((1,), (1,)), ((), ())), preferred_element_type=jnp.float32
    )
    grad_kernel, layer_norm_gain_gradient, grad_ln_bias = lax.psum(
        (
            kernel_portion,
            jnp.sum(normalized_gradient * standardized_input, axis=0),
            jnp.sum(normalized_gradient, axis=0),
        ),
        ("seq", "fsdp"),
    )
    rescaled_rows = normalized_gradient * layer_norm_gain
    input_gradient = row_inverse_deviation * (
        rescaled_rows
        - jnp.mean(rescaled_rows, axis=-1, keepdims=True)
        - standardized_input * jnp.mean(rescaled_rows * standardized_input, axis=-1, keepdims=True)
    )
    row_share = lax.psum_scatter(
        lax.dot_general(
            normalized_rows,
            grad_hidden,
            (((0,), (0,)), ((), ())),
            preferred_element_type=jnp.float32,
        ),
        "fsdp",
        scatter_dimension=0,
        tiled=True,
    )
    grad_w_in = lax.psum(row_share, "seq")
    return (
        output,
        input_gradient.astype(jnp.bfloat16),
        grad_w_in,
        grad_kernel,
        grad_bn_gain,
        grad_bn_bias,
        layer_norm_gain_gradient,
        grad_ln_bias,
    )


def solution(mesh):
    placed = (
        P(("seq", "fsdp"), None),
        P(),
        P(),
        P("fsdp", None),
        P(),
        P(),
        P(),
        P(("seq", "fsdp"), None),
    )
    return jax.shard_map(
        on_device,
        mesh=mesh,
        in_specs=placed,
        out_specs=(
            P(("seq", "fsdp"), None),
            P(("seq", "fsdp"), None),
            P("fsdp", None),
            P(),
            P(),
            P(),
            P(),
            P(),
        ),
        check_vma=False,
    )
```

profile of v0, /device:TPU:0, one launch (start us, length us, event | category | flops | bytes accessed | tf_op | source)
XLA Modules:
  0.0 759.2 jit_solution(17330102155597915595)
XLA Ops:
  7.3 0.7 all-gather.2.cloned.1.call-update
  9.3 67.3 %all-gather.2.cloned.1.call-done = bf16[1536,3072]{1,0:T(8,128)(2,1)} async-done(((bf16[384,3072]{1,0:T(8,128)(2,1)}), bf16[1536,3072]{1,0:T(8,128)(2,1)}) %all-gather.2.cloned.1.call-update) | async-done | bytes 9437200 | tf_op jit(solution)/shard_map/all_gather | solution.py:30
  76.6 6.7 fusion.115
  83.9 1.5 copy-done
  85.5 2.2 collective-permute-start
  87.9 0.7 collective-permute-done
  88.9 10.2 %fusion.119 = (f32[1536]{0:T(1024)S(1)}, f32[384,1536]{1,0:T(8,128)}) fusion(f32[415,1536]{1,0:T(8,128)S(1)} %maximum_convert_fusion, f32[1536]{0:T(1024)S(1)} %get-tuple-element.76, f32[1536]{0:T(1024)S(1)} %get-tuple-element.77, f32[1536]{0:T(1024)S(1)} %get-tuple-element.47, f32[1536]{0:T(1024)S(1)} %get-tuple-element.48, ...), kind=kLoop, calls=%fused_computation.261 | loop fusion | flops 37747200 | bytes 78059520 | tf_op jit(solution)/shard_map/reduce_sum | solution.py:44
  99.1 44.0 %psum.56 = f32[1536]{0:T(1024)S(1)} all-reduce(f32[1536]{0:T(1024)S(1)} %get-tuple-element.85), channel_id=1, replica_groups=mesh['seq'=8,'fsdp'=4] {'seq','fsdp'}, use_global_device_ids=true, to_apply=%region_3.0 | all-reduce | flops 1536 | bytes 12288 | tf_op jit(solution)/shard_map/psum | solution.py:44
  143.2 1.9 multiply_reduce_fusion.33
  145.1 40.1 %psum.57 = f32[1536]{0:T(1024)S(1)} all-reduce(f32[1536]{0:T(1024)S(1)} %multiply_reduce_fusion.33), channel_id=1, replica_groups=mesh['seq'=8,'fsdp'=4] {'seq','fsdp'}, use_global_device_ids=true, to_apply=%region_5.0 | all-reduce | flops 1536 | bytes 12288 | tf_op jit(solution)/shard_map/psum | solution.py:46
  185.3 4.5 fusion.117
  189.7 40.2 %all-reduce.1 = (f32[1536]{0:T(1024)S(1)}, f32[1536]{0:T(1024)S(1)}) all-reduce(f32[1536]{0:T(1024)S(1)} %get-tuple-element.41, f32[1536]{0:T(1024)S(1)} %get-tuple-element.40), channel_id=1, replica_groups=mesh['seq'=8,'fsdp'=4] {'seq','fsdp'}, use_global_device_ids=true, to_apply=%region_9.0 | all-reduce | flops 3072 | bytes 24576 | tf_op jit(solution)/shard_map/psum | solution.py:53
  230.5 8.2 %multiply_reduce_fusion = (f32[1536]{0:T(1024)S(1)}, f32[1536]{0:T(1024)S(1)}, f32[1536]{0:T(1024)S(1)}, f32[1536]{0:T(1024)S(1)}, f32[1536]{0:T(1024)S(1)}, /*i...) fusion(f32[415,1536]{1,0:T(8,128)S(1)} %maximum_convert_fusion,, ...), kind=kLoop, calls=%fused_computation.169 | loop fusion | flops 31822848 | bytes 48519168 | tf_op jit(solution)/shard_map/reduce_sum | solution.py:66
  238.8 1.4 copy-done.1
  240.2 1.5 collective-permute-start.1
  241.7 1.9 collective-permute-done.1
  243.5 40.4 %multiply_convert_fusion.1 = (bf16[384,1536]{1,0:T(8,128)(2,1)S(1)}, f32[384,1536]{1,0:T(8,128)}) fusion(f32[384,3072]{1,0:T(8,128)} %copy-done, f32[31,1536]{1,0:T(8,128)S(1)} %collective-permute-done.1, f32[384,1536]{1,0:T(8,128)} %copy-done.1, f32[1536]{0:T(1024)S(1)} %get-tuple-element.76, f32[1536]{0:T(1024)S(1)} %get-tuple-element.77, ...), kind=kLoop, calls=%fused_computation.202 | loop fusion | flops 58392576 | bytes 8644608 | tf_op jit(solution)/shard_map/convert
  284.0 4.4 multiply_convert_fusion
  288.4 1.0 copy-done.7
  289.4 9.4 %fusion.109 = f32[1536,3072]{1,0:T(8,128)} fusion(bf16[384,1536]{1,0:T(8,128)(2,1)S(1)} %multiply_convert_fusion, bf16[384,1536]{1,0:T(8,128)(2,1)S(1)} %get-tuple-element.83, bf16[384,1536]{1,0:T(8,128)(2,1)S(1)} %copy-done.3, f32[1536]{0:T(1024)S(1)} %copy-done.12, f32[1536]{0:T(1024)S(1)} %copy-done.11, f32[384]{0:T(512)S(1)} %add_rsqrt_fusion.1, ...), kind=kOutput, calls=%fused_computation.214 | convolution fusion | flops 3632136192 | bytes 22428672 | tf_op jit(solution)/shard_map/dot_general | solution.py:94
  298.9 5.4 multiply_reduce_fusion.18
  304.8 2.8 stack.131
  307.9 134.5 %reduce-scatter.2.cloned.1.call-done = f32[384,3072]{1,0:T(8,128)} async-done(((f32[1536,3072]{1,0:T(8,128)}), f32[384,3072]{1,0:T(8,128)}) %reduce-scatter.2.cloned.1.call-update) | async-done | bytes 4718608 | tf_op jit(solution)/shard_map/reduce_scatter | solution.py:93
  442.4 1.2 copy-done.4
  444.3 10.0 %fusion.12 = (f32[1536]{0:T(1024)}, f32[384]{0:T(512)}, f32[384]{0:T(512)}, f32[1536]{0:T(1024)}, f32[384,1536]{1,0:T(8,128)}) fusion(bf16[384,1536]{1,0:T(8,128)(2,1)S(1)} %copy-done.4, f32[384]{0:T(512)S(1)} %add_rsqrt_fusion.1, f32[384]{0:T(512)S(1)} %broadcast_multiply_fusion.4, f32[1536]{0:T(1024)S(1)} %copy-done.11, ...), kind=kOutput, calls=%fused_computation.44 | convolution fusion | flops 3634491392 | bytes 15360000 | tf_op jit(solution)/shard_map/dot_general | solution.py:76
  454.3 39.7 %all-reduce = (f32[1536]{0:T(1024)}, f32[1536]{0:T(1024)}) all-reduce(f32[1536]{0:T(1024)} %get-tuple-element.42, f32[1536]{0:T(1024)} %get-tuple-element.45), channel_id=1, replica_groups=mesh['seq'=8,'fsdp'=4] {'seq','fsdp'}, use_global_device_ids=true, to_apply=%region_48.0 | all-reduce | flops 3072 | bytes 24576 | tf_op jit(solution)/shard_map/psum | solution.py:79
  494.0 0.7 broadcast_multiply_fusion.2
  494.7 3.4 fusion.11
  498.1 74.3 %all-reduce.7.cloned.1.call-done = f32[32,1536]{1,0:T(8,128)} async-done(((f32[32,1536]{1,0:T(8,128)}), f32[32,1536]{1,0:T(8,128)}) %all-reduce.7.cloned.1.call-update) | async-done | bytes 196624 | tf_op jit(solution)/shard_map/psum | solution.py:79
  572.4 174.5 %all-reduce.5.cloned.1.call-done = f32[384,3072]{1,0:T(8,128)} async-done(((f32[384,3072]{1,0:T(8,128)}), f32[384,3072]{1,0:T(8,128)}) %all-reduce.5.cloned.1.call-update) | async-done | bytes 4718608 | tf_op jit(solution)/shard_map/psum | solution.py:104
  746.9 5.1 copy.18
  752.0 0.7 copy.19
  (82 shorter events, 4.5 us)
Async XLA Ops:
  7.2 0.9 copy-start.10
  7.2 1.4 copy-start.2
  7.2 69.4 %copy-start.11 = (f32[1536]{0:T(1024)S(1)}, f32[1536]{0:T(1024)}, u32[]{:S(2)}) copy-start(f32[1536]{0:T(1024)} %param.9) | copy-start | bytes 18436
  7.2 69.4 %copy-start.12 = (f32[1536]{0:T(1024)S(1)}, f32[1536]{0:T(1024)}, u32[]{:S(2)}) copy-start(f32[1536]{0:T(1024)} %param.10) | copy-start | bytes 18436
  7.2 69.4 %all-gather.2.cloned.1.call-start = ((), (), s32[]{:S(2)}) async-start(), calls=%async_computation.1 | async-start | bytes 11796480 | tf_op jit(solution)/shard_map/all_gather | solution.py:30
  7.9 434.4 %reduce-scatter.2.cloned.1.call-start = ((), (), s32[]{:S(2)}) async-start(), calls=%async_computation.2 | async-start | bytes 23592960 | tf_op jit(solution)/shard_map/reduce_scatter | solution.py:93
  83.2 2.2 copy-start
  85.5 3.1 collective-permute-start
  99.1 86.1 %copy-start.13 = (f32[1536]{0:T(1024)S(1)}, f32[1536]{0:T(1024)}, u32[]{:S(2)}) copy-start(f32[1536]{0:T(1024)} %param.13) | copy-start | bytes 18436
  99.1 86.1 %copy-start.14 = (f32[1536]{0:T(1024)S(1)}, f32[1536]{0:T(1024)}, u32[]{:S(2)}) copy-start(f32[1536]{0:T(1024)} %param.14) | copy-start | bytes 18436
  229.9 0.6 copy-start.16
  229.9 8.9 %copy-start.15 = (f32[1536]{0:T(1024)}, f32[1536]{0:T(1024)S(1)}, u32[]{:S(2)}) copy-start(f32[1536]{0:T(1024)S(1)} %get-tuple-element.97) | copy-start | bytes 18436
  238.8 1.4 copy-start.1
  240.2 3.3 collective-permute-start.1
  283.9 4.5 copy-start.5
  283.9 5.5 copy-start.3
  288.4 1.0 copy-start.7
  298.8 273.6 %all-reduce.7.cloned.1.call-start = ((), (), s32[]{:S(2)}) async-start(), calls=%async_computation.4 | async-start | bytes 393216 | tf_op jit(solution)/shard_map/psum | solution.py:79
  307.6 439.3 %all-reduce.5.cloned.1.call-start = ((), (), s32[]{:S(2)}) async-start(), calls=%async_computation.3 | async-start | bytes 9437184 | tf_op jit(solution)/shard_map/psum | solution.py:104
  442.4 1.3 copy-start.4
  442.4 1.6 copy-start.6
  442.4 2.0 copy-start.8
  746.9 5.1 copy-start.9
Sparse Core Ops, SparseCore 0:
  9.6 66.9 all-gather.1
  298.9 143.3 reduce-scatter.1
  449.4 122.9 all-reduce.6
  576.3 170.5 all-reduce.4
where the time goes:
time: 760 us; the launch traced here: 759 us
  waiting for transfers between devices  454 us (60%)
  blocking collectives  164 us (22%)
  other arithmetic  80.9 us (11%)
  matrix products  26 us (3%)
  local copies, waits for them, and re-layouts  16.1 us (2%)
  between operations  14.2 us (2%)
    psum x1, waiting for transfers between devices, on_device(): grad_w_in = lax.psum(row_share, 'seq')  174 us
    reduce_scatter x1, waiting for transfers between devices, on_device(): lax.psum_scatter(lax.dot_general(normalized_rows, grad_hidden, (((0,), (0...  135 us
    psum x1, waiting for transfers between devices, on_device(): lax.psum((kernel_portion, jnp.sum(normalized_gradient * standardized_inpu...  74.3 us
    all_gather x1, waiting for transfers between devices, on_device(): full_weight = lax.all_gather(w_in, 'fsdp', axis=0, tiled=True)  67.3 us
    another operation x2, other arithmetic  44.8 us
    psum x1, blocking collectives, on_device(): lax.psum(jnp.sum(conv_out, axis=0), ('seq', 'fsdp')) / all_frames  44 us
    psum x1, blocking collectives, on_device(): lax.psum((jnp.sum(grad_z, axis=0), jnp.sum(grad_z * chat, axis=0)), ('seq...  40.2 us
    psum x1, blocking collectives, on_device(): lax.psum(jnp.sum(conv_centred * conv_centred, axis=0), ('seq', 'fsdp'))  40.1 us
  transfers between devices with their start and end apart: 6, of which 6 were waited for; matrix products, arithmetic and copies ran while one was open for 3% of the time, Pallas kernels for 0%

commit v1 on v0

--- a/solution.py
+++ b/solution.py
@@ -4,6 +4,18 @@
 from jax.sharding import PartitionSpec as P
 
 epsilon = 1e-05
+
+
+def gather_by_bits(value, axis, dim):
+    ways, here = (lax.axis_size(axis), lax.axis_index(axis))
+    grown, reach = (value, 1)
+    while reach < ways:
+        theirs = lax.ppermute(grown, axis, [(d, d ^ reach) for d in range(ways)])
+        mine_first = jnp.concatenate([grown, theirs], axis=dim)
+        theirs_first = jnp.concatenate([theirs, grown], axis=dim)
+        grown = jnp.where(here & reach == 0, mine_first, theirs_first)
+        reach = 2 * reach
+    return grown
 
 
 def from_behind(block, axis, distance):
@@ -27,7 +39,7 @@
     )
     standardized_input = centered_rows * row_inverse_deviation
     normalized_rows = (standardized_input * layer_norm_gain + layer_norm_bias).astype(jnp.bfloat16)
-    full_weight = lax.all_gather(w_in, "fsdp", axis=0, tiled=True)
+    full_weight = gather_by_bits(w_in, "fsdp", 0)
     hidden = jnp.dot(normalized_rows, full_weight, preferred_element_type=jnp.float32)
     value_part = hidden[:, :features]
     gate_sig = jax.nn.sigmoid(hidden[:, features:])

time: 760 us -> 735 us (0.967)
  waiting for transfers between devices: 454 us -> 407 us
  other arithmetic: 80.9 us -> 89.6 us
    ppermute x0 -> x2, waiting for transfers between devices: none -> 104 us  [gather_by_bits(): theirs = lax.ppermute(grown, axis, [(d, d ^ reach) for d in range(ways)])]
    psum x1, waiting for transfers between devices: 74.3 us -> 0.01 us  [on_device(): lax.psum((kernel_portion, jnp.sum(normalized_gradient * standardized_inpu...]
    all_gather x1 -> x0, waiting for transfers between devices: 67.3 us -> none  [on_device(): full_weight = lax.all_gather(w_in, 'fsdp', axis=0, tiled=True)]
    psum x1, waiting for transfers between devices: 174 us -> 166 us  [on_device(): grad_w_in = lax.psum(row_share, 'seq')]
  transfers between devices with their start and end apart: 6 -> 7, of which waited for: 6 -> 5; matrix products, arithmetic and copies ran while one was open for 3% -> 4% of each run, Pallas kernels for 0% -> 0%
where the time goes in v1:
time: 735 us; the launch traced here: 734 us
  waiting for transfers between devices  407 us (55%)
  blocking collectives  164 us (22%)
  other arithmetic  89.6 us (12%)
  matrix products  31.6 us (4%)
  local copies, waits for them, and re-layouts  18.9 us (3%)
  between operations  15.9 us (2%)
    psum x1, waiting for transfers between devices, on_device(): grad_w_in = lax.psum(row_share, 'seq')  166 us
    reduce_scatter x1, waiting for transfers between devices, on_device(): lax.psum_scatter(lax.dot_general(normalized_rows, grad_hidden, (((0,), (0...  135 us
    ppermute x2, waiting for transfers between devices, gather_by_bits(): theirs = lax.ppermute(grown, axis, [(d, d ^ reach) for d in range(ways)])  104 us
    another operation x2, other arithmetic  46.8 us
    psum x1, blocking collectives, on_device(): lax.psum(jnp.sum(conv_out, axis=0), ('seq', 'fsdp')) / all_frames  44.4 us
    psum x1, blocking collectives, on_device(): lax.psum(jnp.sum(conv_centred * conv_centred, axis=0), ('seq', 'fsdp'))  40.4 us
    psum x1, blocking collectives, on_device(): lax.psum((jnp.sum(grad_z, axis=0), jnp.sum(grad_z * chat, axis=0)), ('seq...  40 us
    psum x1, blocking collectives, on_device(): lax.psum((kernel_portion, jnp.sum(normalized_gradient * standardized_inpu...  39.6 us
  transfers between devices with their start and end apart: 7, of which 5 were waited for; matrix products, arithmetic and copies ran while one was open for 4% of the time, Pallas kernels for 0%

profile of v1, /device:TPU:0, one launch (start us, length us, event | category | flops | bytes accessed | tf_op | source)
XLA Modules:
  0.0 734.2 jit_solution(17657199473934419323)
XLA Ops:
  8.6 4.4 collective-permute-done
  12.9 6.7 maximum_select_fusion.1
  19.6 2.9 collective-permute-start.1
  22.5 2.0 slice_reduce_fusion.31
  25.2 99.7 %collective-permute-done.1 = bf16[768,3072]{1,0:T(8,128)(2,1)} collective-permute-done((bf16[768,3072]{1,0:T(8,128)(2,1)}, bf16[768,3072]{1,0:T(8,128)(2,1)}, u32[]{:S(2)}, u32[]{:S(2)}) %collective-permute-start.1) | collective-permute-done | bytes 4718624 | tf_op jit(solution)/shard_map/ppermute | solution.py:13
  124.9 9.6 %fusion.110 = f32[384,3072]{1,0:T(8,128)S(1)} fusion(bf16[768,3072]{1,0:T(8,128)(2,1)} %collective-permute-done.1, bf16[768,3072]{1,0:T(8,128)(2,1)} %maximum_select_fusion.1, pred[]{:T(512)S(6)} %eq.6, bf16[384,1536]{1,0:T(8,128)(2,1)S(1)} %copy-done.2, f32[1536]{0:T(1024)S(1)} %copy-done.11, f32[1536]{0:T(1024)S(1)} %copy-done.10, ...), kind=kOutput, calls=%fused_computation.217 | convolution fusion | flops 3669884928 | bytes 15350785 | tf_op jit(solution)/shard_map/dot_general | solution.py:43
  135.2 1.5 copy-done
  136.7 1.6 collective-permute-start.2
  138.3 1.5 slice_reduce_fusion.30
  140.2 10.2 %fusion.120 = (f32[1536]{0:T(1024)S(1)}, f32[384,1536]{1,0:T(8,128)}) fusion(f32[415,1536]{1,0:T(8,128)S(1)} %maximum_convert_fusion, f32[1536]{0:T(1024)S(1)} %get-tuple-element.76, f32[1536]{0:T(1024)S(1)} %get-tuple-element.77, f32[1536]{0:T(1024)S(1)} %get-tuple-element.47, f32[1536]{0:T(1024)S(1)} %get-tuple-element.48, ...), kind=kLoop, calls=%fused_computation.264 | loop fusion | flops 37747200 | bytes 78059520 | tf_op jit(solution)/shard_map/reduce_sum | solution.py:56
  150.5 44.4 %psum.56 = f32[1536]{0:T(1024)S(1)} all-reduce(f32[1536]{0:T(1024)S(1)} %get-tuple-element.85), channel_id=1, replica_groups=mesh['seq'=8,'fsdp'=4] {'seq','fsdp'}, use_global_device_ids=true, to_apply=%region_3.4 | all-reduce | flops 1536 | bytes 12288 | tf_op jit(solution)/shard_map/psum | solution.py:56
  194.9 1.9 multiply_reduce_fusion.33
  196.8 40.4 %psum.57 = f32[1536]{0:T(1024)S(1)} all-reduce(f32[1536]{0:T(1024)S(1)} %multiply_reduce_fusion.33), channel_id=1, replica_groups=mesh['seq'=8,'fsdp'=4] {'seq','fsdp'}, use_global_device_ids=true, to_apply=%region_5.6 | all-reduce | flops 1536 | bytes 12288 | tf_op jit(solution)/shard_map/psum | solution.py:58
  237.2 4.5 fusion.118
  241.7 40.0 %all-reduce.1 = (f32[1536]{0:T(1024)S(1)}, f32[1536]{0:T(1024)S(1)}) all-reduce(f32[1536]{0:T(1024)S(1)} %get-tuple-element.41, f32[1536]{0:T(1024)S(1)} %get-tuple-element.40), channel_id=1, replica_groups=mesh['seq'=8,'fsdp'=4] {'seq','fsdp'}, use_global_device_ids=true, to_apply=%region_9.10 | all-reduce | flops 3072 | bytes 24576 | tf_op jit(solution)/shard_map/psum | solution.py:65
  282.3 8.2 %multiply_reduce_fusion = (f32[1536]{0:T(1024)S(1)}, f32[1536]{0:T(1024)S(1)}, f32[1536]{0:T(1024)S(1)}, f32[1536]{0:T(1024)S(1)}, f32[1536]{0:T(1024)S(1)}, /*i...) fusion(f32[415,1536]{1,0:T(8,128)S(1)} %maximum_convert_fusion,, ...), kind=kLoop, calls=%fused_computation.171 | loop fusion | flops 31822848 | bytes 48519168 | tf_op jit(solution)/shard_map/reduce_sum | solution.py:78
  290.6 1.5 copy-done.1
  292.1 1.3 collective-permute-start.3
  293.4 2.0 collective-permute-done.3
  295.4 42.4 %multiply_convert_fusion.1 = (bf16[384,1536]{1,0:T(8,128)(2,1)S(1)}, f32[384,1536]{1,0:T(8,128)}) fusion(f32[384,3072]{1,0:T(8,128)} %copy-done, f32[31,1536]{1,0:T(8,128)S(1)} %collective-permute-done.3, f32[384,1536]{1,0:T(8,128)} %copy-done.1, f32[1536]{0:T(1024)S(1)} %get-tuple-element.76, f32[1536]{0:T(1024)S(1)} %get-tuple-element.77, ...), kind=kLoop, calls=%fused_computation.204 | loop fusion | flops 58392576 | bytes 8644608 | tf_op jit(solution)/shard_map/convert
  337.8 4.4 multiply_convert_fusion
  342.3 1.0 copy-done.7
  343.3 9.4 %fusion.111 = f32[1536,3072]{1,0:T(8,128)} fusion(bf16[384,1536]{1,0:T(8,128)(2,1)S(1)} %multiply_convert_fusion, bf16[384,1536]{1,0:T(8,128)(2,1)S(1)} %get-tuple-element.83, bf16[384,1536]{1,0:T(8,128)(2,1)S(1)} %copy-done.3, f32[1536]{0:T(1024)S(1)} %copy-done.11, f32[1536]{0:T(1024)S(1)} %copy-done.10, f32[384]{0:T(512)S(1)} %add_rsqrt_fusion.1, ...), kind=kOutput, calls=%fused_computation.218 | convolution fusion | flops 3632136192 | bytes 22428672 | tf_op jit(solution)/shard_map/dot_general | solution.py:106
  352.8 5.4 multiply_reduce_fusion.18
  358.7 2.8 stack.131
  361.7 135.2 %reduce-scatter.2.cloned.1.call-done = f32[384,3072]{1,0:T(8,128)} async-done(((f32[1536,3072]{1,0:T(8,128)}), f32[384,3072]{1,0:T(8,128)}) %reduce-scatter.2.cloned.1.call-update) | async-done | bytes 4718608 | tf_op jit(solution)/shard_map/reduce_scatter | solution.py:105
  497.0 1.2 copy-done.4
  498.9 12.5 %fusion.12 = (f32[1536]{0:T(1024)}, f32[384]{0:T(512)}, f32[384]{0:T(512)}, f32[1536]{0:T(1024)}, f32[384,1536]{1,0:T(8,128)}) fusion(bf16[384,1536]{1,0:T(8,128)(2,1)S(1)} %copy-done.4, f32[384]{0:T(512)S(1)} %add_rsqrt_fusion.1, f32[384]{0:T(512)S(1)} %broadcast_multiply_fusion.4, f32[1536]{0:T(1024)S(1)} %copy-done.10, ...), kind=kOutput, calls=%fused_computation.46 | convolution fusion | flops 3676958720 | bytes 15360001 | tf_op jit(solution)/shard_map/dot_general | solution.py:88
  511.5 39.6 %all-reduce = (f32[1536]{0:T(1024)}, f32[1536]{0:T(1024)}) all-reduce(f32[1536]{0:T(1024)} %get-tuple-element.42, f32[1536]{0:T(1024)} %get-tuple-element.45), channel_id=1, replica_groups=mesh['seq'=8,'fsdp'=4] {'seq','fsdp'}, use_global_device_ids=true, to_apply=%region_48.49 | all-reduce | flops 3072 | bytes 24576 | tf_op jit(solution)/shard_map/psum | solution.py:91
  551.8 3.4 fusion.11
  555.2 165.7 %all-reduce.5.cloned.1.call-done = f32[384,3072]{1,0:T(8,128)} async-done(((f32[384,3072]{1,0:T(8,128)}), f32[384,3072]{1,0:T(8,128)}) %all-reduce.5.cloned.1.call-update) | async-done | bytes 4718608 | tf_op jit(solution)/shard_map/psum | solution.py:116
  721.0 5.1 copy.18
  (82 shorter events, 5.6 us)
Async XLA Ops:
  8.0 488.9 %reduce-scatter.2.cloned.1.call-start = ((), (), s32[]{:S(2)}) async-start(), calls=%async_computation.1 | async-start | bytes 23592960 | tf_op jit(solution)/shard_map/reduce_scatter | solution.py:105
  8.0 4.9 collective-permute-start
  8.6 15.9 %copy-start.2 = (bf16[384,1536]{1,0:T(8,128)(2,1)S(1)}, bf16[384,1536]{1,0:T(8,128)(2,1)}, u32[]{:S(2)}) copy-start(bf16[384,1536]{1,0:T(8,128)(2,1)} %param.8) | copy-start | bytes 3538948
  19.6 105.3 %copy-start.10 = (f32[1536]{0:T(1024)S(1)}, f32[1536]{0:T(1024)}, u32[]{:S(2)}) copy-start(f32[1536]{0:T(1024)} %param.9) | copy-start | bytes 18436
  19.6 105.3 %copy-start.11 = (f32[1536]{0:T(1024)S(1)}, f32[1536]{0:T(1024)}, u32[]{:S(2)}) copy-start(f32[1536]{0:T(1024)} %param.10) | copy-start | bytes 18436
  19.6 105.3 %collective-permute-start.1 = (bf16[768,3072]{1,0:T(8,128)(2,1)}, bf16[768,3072]{1,0:T(8,128)(2,1)}, u32[]{:S(2)}, u32[]{:S(2)}) collective-permute-start(bf16[768,3072]{1,0:T(8,128)(2,1)} %maximum_select_fusion.1), channel_id=1, source_target_pairs={{0,2},{1,3},{2,0},{3,1},{4,6},{5,7},{6,4},{7,5},{8,10},{9,11},{10,... | collective-permute-start | bytes 14155784 | tf_op jit(solution)/shard_map/ppermute | solution.py:13
  134.6 2.1 copy-start
  136.7 3.2 collective-permute-start.2
  150.5 86.7 %copy-start.12 = (f32[1536]{0:T(1024)S(1)}, f32[1536]{0:T(1024)}, u32[]{:S(2)}) copy-start(f32[1536]{0:T(1024)} %param.13) | copy-start | bytes 18436
  150.5 86.8 %copy-start.13 = (f32[1536]{0:T(1024)S(1)}, f32[1536]{0:T(1024)}, u32[]{:S(2)}) copy-start(f32[1536]{0:T(1024)} %param.14) | copy-start | bytes 18436
  281.7 0.6 copy-start.15
  281.7 8.9 %copy-start.14 = (f32[1536]{0:T(1024)}, f32[1536]{0:T(1024)S(1)}, u32[]{:S(2)}) copy-start(f32[1536]{0:T(1024)S(1)} %get-tuple-element.97) | copy-start | bytes 18436
  290.6 1.5 copy-start.1
  292.1 3.3 collective-permute-start.3
  337.8 4.5 copy-start.5
  337.8 5.5 copy-start.3
  342.3 1.0 copy-start.7
  352.7 202.5 %all-reduce.7.cloned.1.call-start = ((), (), s32[]{:S(2)}) async-start(), calls=%async_computation.3 | async-start | bytes 393216 | tf_op jit(solution)/shard_map/psum | solution.py:91
  361.5 359.5 %all-reduce.5.cloned.1.call-start = ((), (), s32[]{:S(2)}) async-start(), calls=%async_computation.2 | async-start | bytes 9437184 | tf_op jit(solution)/shard_map/psum | solution.py:116
  496.9 1.3 copy-start.4
  496.9 1.6 copy-start.6
  496.9 2.0 copy-start.8
  721.0 5.1 copy-start.9
Sparse Core Ops, SparseCore 0:
  352.8 144.0 reduce-scatter.1
Sparse Core Ops, SparseCore 1:
  361.5 185.3 all-reduce.6
  550.8 170.1 all-reduce.4
